TPU v7x, 128 devices: a whole 4x4x4 slice. The times are simulated.
128 devices in a mesh: req: 8 (over z, core), shard: 16 (over x, y).
Axes of the slice: x: 4, y: 4, z: 4, core: 2. Of those that a mesh axis runs over, the one named last changes fastest.
Arguments:
- hidden_states: bfloat16 [16384, 1536], P(('req', 'shard')), may hold values from -6 to 6
- attn_gain: float32 [1536], replicated, may hold values from 0.5 to 1.5
- w_qkv: bfloat16 [1536, 2560], replicated, may hold values from -0.15625 to 0.15625
- w_out: bfloat16 [1536, 1536], replicated, may hold values from -0.15625 to 0.15625
- kv_cache: bfloat16 [8, 4096, 1024], P('req', 'shard'), may hold values from -80 to 80, as said below
- cached_len: int32 [8], P('req'), may hold values from 128 to 4096, as said below
- ffn_gain: float32 [1536], replicated, may hold values from 0.5 to 1.5
- w_router: bfloat16 [1536, 40], replicated, may hold values from -0.15625 to 0.15625
- expert_ids: int32 [16384, 8], P(('req', 'shard')), may hold values from 0 to 39, all different within a row; in each aligned block of 128 rows (0 to 127, 128 to 255, ...) at most 32 rows name the same one
- w_gate: bfloat16 [40, 512, 1536], P('req', 'shard'), may hold values from -0.15625 to 0.15625
- w_up: bfloat16 [40, 512, 1536], P('req', 'shard'), may hold values from -0.15625 to 0.15625
- w_down: bfloat16 [40, 512, 1536], P('req', 'shard'), may hold values from -0.25 to 0.25
Outputs:
- layer_out: bfloat16 [16384, 1536], P(('req', 'shard'))
Inputs may be any that keep to these rules, and one draw needn't show every extreme that they name: `cached_len`: each request's length is drawn either between 128 and 512 or between 3072 and 4096; some request has exactly 4096. `expert_ids`: among the 128 rows of one device no expert is named by more than 32 rows. `kv_cache`: cached keys and values, already rotated.
All inputs are finite; a program needn't handle non-finite values.
Results may differ from a plain program's by a relative error of at most 0.025.
Values may be sent and summed in bfloat16 or wider, within the bound.
No kernel may reach another device: no remote copies, remote signals or barrier semaphores. Data moves between devices by JAX's collectives and lax.ppermute only.
A program may use at most 192 MiB of HBM per device.

v0:
```python
import math
import jax
import jax.numpy as jnp
from jax import lax
from jax.sharding import PartitionSpec as P

D = 1536
HEADS = 24
KVH = 8
HD = 64
TOP = 8
EPSILON = 1e-05
NEG_FILL = -1e30
FAR_LIMIT = 1 << 30


def rms_scale(values, gain):
    floats = values.astype(jnp.float32)
    inverse = lax.rsqrt(jnp.mean(floats * floats, axis=-1, keepdims=True) + EPSILON)
    return (floats * inverse * gain).astype(jnp.bfloat16)


def rotate(values, positions):
    half_dim = values.shape[-1] // 2
    freqs = jnp.power(10000.0, -jnp.arange(half_dim, dtype=jnp.float32) / half_dim)
    angles = positions.astype(jnp.float32)[:, None] * freqs[None, :]
    cosine = jnp.cos(angles)[:, None, :]
    sine = jnp.sin(angles)[:, None, :]
    first = values[..., :half_dim]
    second = values[..., half_dim:]
    return jnp.concatenate(
        [first * cosine - second * sine, second * cosine + first * sine], axis=-1
    )


def empty_state(rows):
    groups = HEADS // KVH
    return (
        jnp.full((rows, KVH, groups), NEG_FILL, jnp.float32),
        jnp.zeros((rows, KVH, groups), jnp.float32),
        jnp.zeros((rows, KVH, groups, HD), jnp.float32),
    )


def attend_block(state, queries, query_pos, block, key_pos, key_limit):
    max_run, total, accum = state
    rows = block.shape[0]
    keys = block[:, : KVH * HD].reshape(rows, KVH, HD)
    values = block[:, KVH * HD :].reshape(rows, KVH, HD)
    scores = jnp.einsum(
        "tgqd,rgd->tgqr", queries, keys, preferred_element_type=jnp.float32
    ) * HD ** (-0.5)
    allowed = (key_pos[None, :] <= query_pos[:, None]) & (key_pos < key_limit)[None, :]
    allowed = allowed[:, None, None, :]
    block_max = jnp.max(jnp.where(allowed, scores, NEG_FILL), axis=-1)
    new_max = jnp.maximum(max_run, block_max)
    weights = jnp.where(allowed, jnp.exp(scores - new_max[..., None]), 0.0)
    factor = jnp.exp(max_run - new_max)
    total = total * factor + jnp.sum(weights, axis=-1)
    accum = accum * factor[..., None] + jnp.einsum(
        "tgqr,rgd->tgqd", weights.astype(jnp.bfloat16), values, preferred_element_type=jnp.float32
    )
    return (new_max, total, accum)


def fold_rows(state, queries, query_pos, piece, key_pos, key_limit):
    rows = piece.shape[0]
    step_rows = math.gcd(rows, 512)
    count = rows // step_rows
    blocks = piece.reshape(count, step_rows, piece.shape[1])
    positions = key_pos.reshape(count, step_rows)

    def advance(carry, item):
        return (attend_block(carry, queries, query_pos, item[0], item[1], key_limit), None)

    state, _ = lax.scan(advance, state, (blocks, positions))
    return state


def local(
    hidden_states,
    attn_gain,
    w_qkv,
    w_out,
    kv_cache,
    cached_len,
    ffn_gain,
    w_router,
    expert_ids,
    w_gate,
    w_up,
    w_down,
):
    groups = HEADS // KVH
    tok_rows = hidden_states.shape[0]
    shard_pos = lax.axis_index("shard")
    length = cached_len[0]
    normed = rms_scale(hidden_states, attn_gain)
    qkv = jnp.dot(normed, w_qkv, preferred_element_type=jnp.float32)
    positions = length + shard_pos * tok_rows + jnp.arange(tok_rows, dtype=jnp.int32)
    queries = rotate(qkv[:, : HEADS * HD].reshape(tok_rows, HEADS, HD), positions).astype(
        jnp.bfloat16
    )
    new_keys = rotate(
        qkv[:, HEADS * HD : (HEADS + KVH) * HD].reshape(tok_rows, KVH, HD), positions
    ).astype(jnp.bfloat16)
    new_values = qkv[:, (HEADS + KVH) * HD :].astype(jnp.bfloat16)
    new_kv = jnp.concatenate([new_keys.reshape(tok_rows, KVH * HD), new_values], axis=1)
    cache_local = kv_cache[0]
    query_heads = queries.reshape(tok_rows, KVH, groups, HD)
    piece = lax.all_gather(cache_local, "shard", axis=0, tiled=True)
    key_pos = jnp.arange(piece.shape[0], dtype=jnp.int32)
    state = fold_rows(empty_state(tok_rows), query_heads, positions, piece, key_pos, length)
    piece = lax.all_gather(new_kv, "shard", axis=0, tiled=True)
    key_pos = length + jnp.arange(piece.shape[0], dtype=jnp.int32)
    max_run, total, accum = fold_rows(state, query_heads, positions, piece, key_pos, FAR_LIMIT)
    attended = (accum / total[..., None]).astype(jnp.bfloat16)
    attended = attended.reshape(tok_rows, HEADS * HD)
    mid = (
        hidden_states.astype(jnp.float32)
        + jnp.dot(attended, w_out, preferred_element_type=jnp.float32)
    ).astype(jnp.bfloat16)
    normed2 = rms_scale(mid, ffn_gain)
    group_count = lax.axis_size("req")
    local_experts = w_gate.shape[0]
    expert_count = local_experts * group_count
    capacity = min(tok_rows, 5 * tok_rows * TOP // (4 * expert_count))
    logits = jnp.dot(normed2, w_router, preferred_element_type=jnp.float32)
    picked = expert_ids[:, :, None] == jnp.arange(expert_count, dtype=jnp.int32)[None, None, :]
    chosen = jnp.sum(jnp.where(picked, logits[:, None, :], 0.0), axis=-1)
    gates = jax.nn.softmax(chosen, axis=-1)
    flat_hot = picked.reshape(tok_rows * TOP, expert_count).astype(jnp.int32)
    ranks = jnp.cumsum(flat_hot, axis=0) - flat_hot
    slot_rank = jnp.sum(ranks * flat_hot, axis=-1)
    slots = expert_ids.reshape(-1) * capacity + slot_rank
    slot_table = (
        slots.reshape(tok_rows, TOP)[:, :, None]
        == jnp.arange(expert_count * capacity, dtype=jnp.int32)[None, None, :]
    )
    placing = jnp.any(slot_table, axis=1).astype(jnp.bfloat16)
    outgoing = jnp.einsum("ts,td->sd", placing, normed2, preferred_element_type=jnp.float32).astype(
        jnp.bfloat16
    )
    outgoing = outgoing.reshape(group_count, local_experts, capacity, D)
    arrived = lax.all_to_all(outgoing, "req", split_axis=0, concat_axis=0, tiled=True)
    weights = jnp.concatenate([w_gate, w_up, w_down], axis=-1)
    weights = lax.all_gather(weights, "shard", axis=1, tiled=True)
    gate_piece = weights[..., :D]
    up_piece = weights[..., D : 2 * D]
    down_piece = weights[..., 2 * D :]
    gate = jnp.einsum("sjcd,jhd->sjch", arrived, gate_piece, preferred_element_type=jnp.float32)
    upper = jnp.einsum("sjcd,jhd->sjch", arrived, up_piece, preferred_element_type=jnp.float32)
    inner = (jax.nn.silu(gate) * upper).astype(jnp.bfloat16)
    summed = jnp.einsum("sjch,jhd->sjcd", inner, down_piece, preferred_element_type=jnp.float32)
    returned = lax.all_to_all(
        summed.astype(jnp.bfloat16), "req", split_axis=0, concat_axis=0, tiled=True
    )
    returned = returned.reshape(expert_count * capacity, D)
    expert_rows = returned[slots].reshape(tok_rows, TOP, D)
    mixture = jnp.sum(gates[:, :, None] * expert_rows.astype(jnp.float32), axis=1)
    return (mid.astype(jnp.float32) + mixture).astype(jnp.bfloat16)


def solution(mesh):
    return jax.shard_map(
        local,
        mesh=mesh,
        in_specs=(
            P(("req", "shard"), None),
            P(),
            P(),
            P(),
            P("req", "shard", None),
            P("req"),
            P(),
            P(),
            P(("req", "shard"), None),
            P("req", "shard", None),
            P("req", "shard", None),
            P("req", "shard", None),
        ),
        out_specs=P(("req", "shard"), None),
        check_vma=False,
    )
```

profile of v0, /device:TPU:1, one launch (start us, length us, event | category | flops | bytes accessed | tf_op | source)
XLA Modules:
  0.0 382.5 jit_solution(826455171912664360)
XLA Ops:
  8.5 4.7 %fusion.60 = f32[128,2560]{1,0:T(8,128)S(1)} fusion(bf16[1536,2560]{1,0:T(8,128)(2,1)} %param.18, bf16[128,1536]{1,0:T(8,128)(2,1)} %param.16, f32[1536]{0:T(1024)} %param.17, f32[128]{0:T(128)S(1)} %add_rsqrt_fusion.1), kind=kOutput, calls=%fused_computation.82 | convolution fusion | flops 1007419392 | bytes 9574912 | tf_op jit(solution)/shard_map/dot_general | solution.py:99
  15.3 2.3 pad_maximum_fusion
  18.0 11.3 %reduce-window.6 = s32[40,8,128]{2,1,0:T(8,128)S(1)} reduce-window(s32[40,8,128]{2,1,0:T(8,128)S(1)} %fusion.67, s32[]{:T(128)} %copy.121), window={size=1x1x128 pad=0_0x0_0x127_0}, to_apply=%region_13.14 | reduce-window | flops 5201920 | bytes 327684 | tf_op jit(solution)/shard_map/reduce-window
  30.3 1.6 fusion.41
  32.0 51.2 %all-gather.9.cloned.1.call-done = bf16[1,4096,1024]{2,1,0:T(8,128)(2,1)} async-done(((bf16[1,256,1024]{2,1,0:T(8,128)(2,1)}), bf16[1,4096,1024]{2,1,0:T(8,128)(2,1)}) %all-gather.9.cloned.1.call-update) | async-done | bytes 8388624 | tf_op jit(solution)/shard_map/all_gather | solution.py:111
  83.2 60.8 %while.31 = (s32[]{:T(128)}, f32[128,8,3]{0,2,1:T(4,128)S(1)}, f32[128,8,3]{0,2,1:T(4,128)S(1)}, f32[128,8,3,64]{0,3,2,1:T(8,128)}, s32[8,512]{1,0:T(8,128)S(1)}...) while((s32[]{:T(128)}, f32[128,8,3]{0,2,1:T(4,128)S(1)}, ...), condition=%wide.region_4.5_spmd.clone, body=%wide.region_1.4_spmd.clone.sunk | while | flops 420691584 | bytes 34939080 | solution.py:76
  88.5 1.4 fusion.119
  111.2 1.4 fusion.119
  118.8 1.4 fusion.119
  126.4 1.4 fusion.119
  134.1 1.4 fusion.119
  141.7 1.4 fusion.119
  144.0 28.0 %while.30 = (s32[]{:T(128)}, f32[128,8,3]{0,2,1:T(4,128)S(1)}, f32[128,8,3]{0,2,1:T(4,128)S(1)}, f32[128,8,3,64]{0,3,2,1:T(8,128)}, s32[4,512]{1,0:T(4,128)S(1)}...) while((s32[]{:T(128)}, f32[128,8,3]{0,2,1:T(4,128)S(1)}, ...), condition=%wide.region_8.9_spmd.clone, body=%wide.region_5.8_spmd.clone.sunk | while | flops 420485760 | bytes 34939048 | solution.py:76
  151.2 1.5 constant_dynamic-slice_fusion.8
  173.3 3.2 multiply_reduce_fusion
  177.8 50.9 %all_to_all.10 = bf16[8,5,32,1536]{3,2,1,0:T(8,128)(2,1)} all-to-all(bf16[8,5,32,1536]{3,2,1,0:T(8,128)(2,1)S(1)} %bitcast.209), channel_id=1, replica_groups=mesh['req'=8,'shard'=16] {'req'}, dimensions={0} | all-to-all | bytes 7864320 | tf_op jit(solution)/shard_map/all_to_all | solution.py:145
  228.7 55.6 %all-gather.7.cloned.1.call-done = bf16[5,512,4608]{2,1,0:T(8,128)(2,1)} async-done(((bf16[5,32,4608]{2,1,0:T(8,128)(2,1)}), bf16[5,512,4608]{2,1,0:T(8,128)(2,1)}) %all-gather.7.cloned.1.call-update) | async-done | bytes 23592976 | tf_op jit(solution)/shard_map/all_gather | solution.py:147
  284.2 8.1 %fusion.38 = f32[5,512,8,32]{1,3,2,0:T(8,128)} fusion(bf16[5,512,4608]{2,1,0:T(8,128)(2,1)} %all-gather.7.cloned.1.call-done, bf16[8,5,32,1536]{3,2,1,0:T(8,128)(2,1)} %all_to_all.10), kind=kOutput, calls=%fused_computation.49 | convolution fusion | flops 2013265920 | bytes 14417920 | tf_op jit(solution)/shard_map/sjcd,jhd->sjch/dot_general | solution.py:151
  292.3 12.6 %fusion.43 = bf16[8,5,32,1536]{3,2,0,1:T(8,128)(2,1)} fusion(bf16[5,512,4608]{2,1,0:T(8,128)(2,1)} %all-gather.7.cloned.1.call-done, f32[5,512,8,32]{1,3,2,0:T(8,128)} %fusion.38, bf16[8,5,32,1536]{3,2,1,0:T(8,128)(2,1)} %all_to_all.10), kind=kOutput, calls=%fused_computation.58 | convolution fusion | flops 4032430080 | bytes 26214400 | tf_op jit(solution)/shard_map/sjch,jhd->sjcd/dot_general | solution.py:154
  304.9 4.5 %copy.70 = bf16[8,5,32,1536]{3,2,1,0:T(8,128)(2,1)} copy(bf16[8,5,32,1536]{3,2,0,1:T(8,128)(2,1)} %fusion.43) | data formatting | bytes 7864320 | tf_op jit(solution)/shard_map/convert_element_type | solution.py:156
  309.3 5.3 %all-to-all-start.1 = ((bf16[8,5,32,1536]{3,2,1,0:T(8,128)(2,1)}), bf16[8,5,32,1536]{3,2,1,0:T(8,128)(2,1)}, u32[]{:S(2)}, u32[]{:S(2)}) async-start(bf16[8,5,32,1536]{3,2,1,0:T(8,128)(2,1)} %copy.70), calls=%async_computation.1 | async-start | bytes 7864320 | tf_op jit(solution)/shard_map/all_to_all | solution.py:155
  315.2 45.3 %all-to-all-done.1 = bf16[8,5,32,1536]{3,2,1,0:T(8,128)(2,1)} async-done(((bf16[8,5,32,1536]{3,2,1,0:T(8,128)(2,1)}), bf16[8,5,32,1536]{3,2,1,0:T(8,128)(2,1)}, u32[]{:S(2)}, u32[]{:S(2)}) %all-to-all-start.1) | async-done | bytes 3932192 | tf_op jit(solution)/shard_map/all_to_all | solution.py:155
  360.5 9.9 %gather_fusion = bf16[1024,1536]{1,0:T(8,128)(2,1)} fusion(bf16[1280,1536]{1,0:T(8,128)(2,1)} %bitcast.21, s32[1024]{0:T(1024)S(1)} %broadcast_clamp_fusion), kind=kCustom, calls=%fused_computation | custom fusion | bytes 6295552 | tf_op jit(solution)/shard_map/gather | solution.py:159
  370.4 4.7 %fusion.40 = f32[128,1536]{1,0:T(8,128)S(1)} fusion(bf16[1024,1536]{1,0:T(8,128)(2,1)} %gather_fusion, f32[128,8]{1,0:T(8,128)S(1)} %copy.62), kind=kLoop, calls=%fused_computation.54 | loop fusion | flops 4521984 | bytes 3936256 | tf_op jit(solution)/shard_map/reduce_sum | solution.py:160
  (251 shorter events, 86.4 us)
Async XLA Ops:
  6.5 308.2 %copy-start = (bf16[1536,40]{0,1:T(8,128)(2,1)S(1)}, bf16[1536,40]{0,1:T(8,128)(2,1)}, u32[]{:S(2)}) copy-start(bf16[1536,40]{0,1:T(8,128)(2,1)} %param.23) | copy-start | bytes 368644
  6.5 76.7 %all-gather.9.cloned.1.call-start = ((), (), s32[]{:S(2)}) async-start(), calls=%async_computation.4 | async-start | bytes 8912896 | tf_op jit(solution)/shard_map/all_gather | solution.py:111
  7.3 136.8 %all-gather.5.cloned.1.call-start = ((), (), s32[]{:S(2)}) async-start(), calls=%async_computation.2 | async-start | bytes 4456448 | tf_op jit(solution)/shard_map/all_gather | solution.py:114
  8.5 6.8 %copy-start.6 = (bf16[5,32,1536]{2,1,0:T(8,128)(2,1)S(1)}, bf16[5,32,1536]{2,1,0:T(8,128)(2,1)}, u32[]{:S(2)}) copy-start(bf16[5,32,1536]{2,1,0:T(8,128)(2,1)} %param.27) | copy-start | bytes 1474564
  8.5 6.8 %copy-start.7 = (bf16[5,32,1536]{2,1,0:T(8,128)(2,1)S(1)}, bf16[5,32,1536]{2,1,0:T(8,128)(2,1)}, u32[]{:S(2)}) copy-start(bf16[5,32,1536]{2,1,0:T(8,128)(2,1)} %param.26) | copy-start | bytes 1474564
  13.2 4.4 %copy-start.9 = (s32[128,8]{0,1:T(8,128)S(1)}, s32[128,8]{0,1:T(8,128)}, u32[]{:S(2)}) copy-start(s32[128,8]{0,1:T(8,128)} %param.24) | copy-start | bytes 12292
  15.2 269.0 %all-gather.7.cloned.1.call-start = ((), (), s32[]{:S(2)}) async-start(), calls=%async_computation.3 | async-start | bytes 25067520 | tf_op jit(solution)/shard_map/all_gather | solution.py:147
  86.0 2.4 copy-start.2
  89.9 0.9 copy-start.3
  93.6 2.4 copy-start.2
  97.5 0.9 copy-start.3
  101.2 2.4 copy-start.2
  108.8 2.4 copy-start.2
  116.4 2.4 copy-start.2
  124.0 2.4 copy-start.2
  131.7 2.4 copy-start.2
  139.2 2.4 copy-start.2
  144.0 29.2 %copy-start.1 = (bf16[128,1536]{1,0:T(8,128)(2,1)S(1)}, bf16[128,1536]{1,0:T(8,128)(2,1)}, u32[]{:S(2)}) copy-start(bf16[128,1536]{1,0:T(8,128)(2,1)} %param.16) | copy-start | bytes 1179652
  146.2 2.4 copy-start.4
  153.3 2.4 copy-start.4
  160.3 2.4 copy-start.4
  167.2 2.4 copy-start.4
  172.0 4.5 %copy-start.8 = (f32[1536]{0:T(1024)S(1)}, f32[1536]{0:T(1024)}, u32[]{:S(2)}) copy-start(f32[1536]{0:T(1024)} %param.22) | copy-start | bytes 18436
  309.3 51.2 %all-to-all-start.1 = ((bf16[8,5,32,1536]{3,2,1,0:T(8,128)(2,1)}), bf16[8,5,32,1536]{3,2,1,0:T(8,128)(2,1)}, u32[]{:S(2)}, u32[]{:S(2)}) async-start(bf16[8,5,32,1536]{3,2,1,0:T(8,128)(2,1)} %copy.70), calls=%async_computation.1 | async-start | bytes 7864320 | tf_op jit(solution)/shard_map/all_to_all | solution.py:155
  (10 other events, 9.1 us)
Sparse Core Ops, SparseCore 0:
  9.5 73.6 all-gather.8
  85.4 51.0 all-gather.4
  138.6 145.6 all-gather.6
where the time goes:
time: 384 us; the launch traced here: 383 us
  waiting for transfers between devices  153 us (40%)
  matrix products  60.4 us (16%)
  blocking collectives  50.9 us (13%)
  local copies, waits for them, and re-layouts  49.9 us (13%)
  other arithmetic  48.2 us (13%)
  between operations  14.1 us (4%)
  starting transfers between devices  5.34 us (1%)
    all_gather x1, waiting for transfers between devices, local(): weights = lax.all_gather(weights, 'shard', axis=1, tiled=True)  55.6 us
    all_gather x1, waiting for transfers between devices, local(): piece = lax.all_gather(cache_local, 'shard', axis=0, tiled=True)  51.2 us
    all_to_all x1, blocking collectives, local(): lax.all_to_all(outgoing, 'req', split_axis=0, concat_axis=0, tiled=True)  50.9 us
    all_to_all x1, waiting for transfers between devices, local(): lax.all_to_all(summed.astype(jnp.bfloat16), 'req', split_axis=0, concat_a...  45.3 us
    dynamic_slice x24, local copies, waits for them, and re-layouts, fold_rows(): state, _ = lax.scan(advance, state, (blocks, positions))  22.4 us
    dot_general x12, matrix products, attend_block(): jnp.einsum('tgqr,rgd->tgqd', weights.astype(jnp.bfloat16), values, prefer...  17.3 us
    reduce_sum x12, other arithmetic, attend_block(): total = total * factor + jnp.sum(weights, axis=-1)  15.3 us
    dot_general x12, matrix products, attend_block(): jnp.einsum('tgqd,rgd->tgqr', queries, keys, preferred_element_type=jnp.fl...  13 us
  transfers between devices with their start and end apart: 4, of which 3 were waited for; matrix products, arithmetic and copies ran while one was open for 28% of the time, Pallas kernels for 0%

commit v1 on v0

--- a/solution.py
+++ b/solution.py
@@ -108,7 +108,9 @@
     new_kv = jnp.concatenate([new_keys.reshape(tok_rows, KVH * HD), new_values], axis=1)
     cache_local = kv_cache[0]
     query_heads = queries.reshape(tok_rows, KVH, groups, HD)
-    piece = lax.all_gather(cache_local, "shard", axis=0, tiled=True)
+    piece = jnp.concatenate(
+        lax.all_to_all(jnp.stack([cache_local] * lax.axis_size("shard")), "shard", 0, 0), axis=0
+    )
     key_pos = jnp.arange(piece.shape[0], dtype=jnp.int32)
     state = fold_rows(empty_state(tok_rows), query_heads, positions, piece, key_pos, length)
     piece = lax.all_gather(new_kv, "shard", axis=0, tiled=True)

time: 384 us -> 474 us (1.23)
  other arithmetic: 48.2 us -> 72.3 us
  waiting for transfers between devices: 153 us -> 177 us
  matrix products: 60.4 us -> 83.1 us
  starting transfers between devices: 5.34 us -> 13.4 us
  local copies, waits for them, and re-layouts: 49.9 us -> 57.6 us
    all_to_all x0 -> x1, waiting for transfers between devices: none -> 132 us  [local(): lax.all_to_all(jnp.stack([cache_local] * lax.axis_size('shard')), 'shard'...]
    all_gather x1, waiting for transfers between devices: 55.6 us -> 0.01 us  [local(): weights = lax.all_gather(weights, 'shard', axis=1, tiled=True)]
    all_gather x1 -> x0, waiting for transfers between devices: 51.2 us -> none  [local(): piece = lax.all_gather(cache_local, 'shard', axis=0, tiled=True)]
    reduce_sum x12, other arithmetic: 15.3 us -> 40.4 us  [attend_block(): total = total * factor + jnp.sum(weights, axis=-1)]
    dot_general x12, matrix products: 13 us -> 35.4 us  [attend_block(): jnp.einsum('tgqd,rgd->tgqr', queries, keys, preferred_element_type=jnp.fl...]
    all_to_all x0 -> x1, starting transfers between devices: none -> 7.77 us  [local(): lax.all_to_all(jnp.stack([cache_local] * lax.axis_size('shard')), 'shard'...]
    while x60 -> x76, local copies, waits for them, and re-layouts: 10.8 us -> 14.3 us
  transfers between devices with their start and end apart: 4 -> 4, of which waited for: 3 -> 2; matrix products, arithmetic and copies ran while one was open for 28% -> 32% of each run, Pallas kernels for 0% -> 0%
where the time goes in v1:
time: 474 us; the launch traced here: 473 us
  waiting for transfers between devices  177 us (37%)
  matrix products  83.1 us (18%)
  other arithmetic  72.3 us (15%)
  local copies, waits for them, and re-layouts  57.6 us (12%)
  blocking collectives  54.3 us (11%)
  between operations  14.4 us (3%)
  starting transfers between devices  13.4 us (3%)
    all_to_all x1, waiting for transfers between devices, local(): lax.all_to_all(jnp.stack([cache_local] * lax.axis_size('shard')), 'shard'...  132 us
    all_to_all x1, blocking collectives, local(): lax.all_to_all(outgoing, 'req', split_axis=0, concat_axis=0, tiled=True)  54.3 us
    all_to_all x1, waiting for transfers between devices, local(): lax.all_to_all(summed.astype(jnp.bfloat16), 'req', split_axis=0, concat_a...  45.4 us
    reduce_sum x12, other arithmetic, attend_block(): total = total * factor + jnp.sum(weights, axis=-1)  40.4 us
    dot_general x12, matrix products, attend_block(): jnp.einsum('tgqd,rgd->tgqr', queries, keys, preferred_element_type=jnp.fl...  35.4 us
    dynamic_slice x24, local copies, waits for them, and re-layouts, fold_rows(): state, _ = lax.scan(advance, state, (blocks, positions))  22.4 us
    dot_general x12, matrix products, attend_block(): jnp.einsum('tgqr,rgd->tgqd', weights.astype(jnp.bfloat16), values, prefer...  17.5 us
    while x76, local copies, waits for them, and re-layouts  14.3 us
  transfers between devices with their start and end apart: 4, of which 2 were waited for; matrix products, arithmetic and copies ran while one was open for 32% of the time, Pallas kernels for 0%

profile of v1, /device:TPU:1, one launch (start us, length us, event | category | flops | bytes accessed | tf_op | source)
XLA Modules:
  0.0 473.1 jit_solution(8992146433690560215)
XLA Ops:
  7.8 4.7 fusion.60
  14.4 4.3 stack.3
  18.8 7.8 %all-to-all-start = ((bf16[16,256,1024]{2,1,0:T(8,128)(2,1)}), bf16[16,256,1024]{2,1,0:T(8,128)(2,1)}, u32[]{:S(2)}, u32[]{:S(2)}) async-start(bf16[16,256,1024]{2,1,0:T(8,128)(2,1)} %stack.3), calls=%async_computation | async-start | bytes 16777216 | tf_op jit(solution)/shard_map/all_to_all | solution.py:112
  28.7 11.3 %reduce-window.6 = s32[40,8,128]{2,1,0:T(8,128)S(1)} reduce-window(s32[40,8,128]{2,1,0:T(8,128)S(1)} %fusion.67, s32[]{:T(128)} %copy.121), window={size=1x1x128 pad=0_0x0_0x127_0}, to_apply=%region_13.14 | reduce-window | flops 5201920 | bytes 327684 | tf_op jit(solution)/shard_map/reduce-window
  42.5 131.8 %all-to-all-done = bf16[16,256,1024]{2,1,0:T(8,128)(2,1)} async-done(((bf16[16,256,1024]{2,1,0:T(8,128)(2,1)}), bf16[16,256,1024]{2,1,0:T(8,128)(2,1)}, u32[]{:S(2)}, u32[]{:S(2)}) %all-to-all-start) | async-done | bytes 8388640 | tf_op jit(solution)/shard_map/all_to_all | solution.py:112
  174.3 111.8 %while.31 = (s32[]{:T(128)}, f32[128,8,3]{0,2,1:T(4,128)S(1)}, f32[128,8,3]{0,2,1:T(4,128)S(1)}, f32[128,8,3,64]{0,3,2,1:T(8,128)}, s32[8,512]{1,0:T(8,128)S(1)}...) while((s32[]{:T(128)}, f32[128,8,3]{0,2,1:T(4,128)S(1)}, ...), condition=%wide.region_4.5_spmd.clone, body=%wide.region_1.4_spmd.clone.sunk | while | flops 420691584 | bytes 60104932 | solution.py:76
  180.9 4.2 fusion.117
  194.5 5.1 %fusion.117 = f32[128,8,3]{0,2,1:T(4,128)S(1)} fusion(f32[8,512,128,3]{2,1,3,0:T(8,128)} %get-tuple-element.405, f32[128,8,3]{0,2,1:T(4,128)S(1)} %select_maximum_fusion.2, pred[128,512]{0,1:T(8,128)(4,1)S(1)} %compare_and_fusion.5), kind=kLoop, calls=%fused_computation.29.clone.1 | loop fusion | flops 6288384 | bytes 6381568 | tf_op jit(solution)/shard_map/while/body/eval_jaxpr/reduce_sum | solution.py:59
  209.6 4.4 fusion.117
  223.4 4.2 fusion.117
  233.2 4.5 fusion.116
  237.8 4.2 fusion.117
  251.4 4.3 fusion.117
  265.3 4.2 fusion.117
  279.0 4.4 fusion.117
  286.1 28.1 %while.30 = (s32[]{:T(128)}, f32[128,8,3]{0,2,1:T(4,128)S(1)}, f32[128,8,3]{0,2,1:T(4,128)S(1)}, f32[128,8,3,64]{0,3,2,1:T(8,128)}, s32[4,512]{1,0:T(4,128)S(1)}...) while((s32[]{:T(128)}, f32[128,8,3]{0,2,1:T(4,128)S(1)}, ...), condition=%wide.region_8.9_spmd.clone, body=%wide.region_5.8_spmd.clone.sunk | while | flops 420485760 | bytes 34939048 | solution.py:76
  320.0 54.3 %all_to_all.15 = bf16[8,5,32,1536]{3,2,1,0:T(8,128)(2,1)} all-to-all(bf16[8,5,32,1536]{3,2,1,0:T(8,128)(2,1)S(1)} %bitcast.210), channel_id=1, replica_groups=mesh['req'=8,'shard'=16] {'req'}, dimensions={0} | all-to-all | bytes 7864320 | tf_op jit(solution)/shard_map/all_to_all | solution.py:147
  374.3 8.1 %fusion.38 = f32[5,512,8,32]{1,3,2,0:T(8,128)} fusion(bf16[5,512,4608]{2,1,0:T(8,128)(2,1)} %all-gather.5.cloned.1.call-done, bf16[8,5,32,1536]{3,2,1,0:T(8,128)(2,1)} %all_to_all.15), kind=kOutput, calls=%fused_computation.49 | convolution fusion | flops 2013265920 | bytes 14417920 | tf_op jit(solution)/shard_map/sjcd,jhd->sjch/dot_general | solution.py:153
  382.4 12.6 %fusion.43 = bf16[8,5,32,1536]{3,2,0,1:T(8,128)(2,1)} fusion(bf16[5,512,4608]{2,1,0:T(8,128)(2,1)} %all-gather.5.cloned.1.call-done, f32[5,512,8,32]{1,3,2,0:T(8,128)} %fusion.38, bf16[8,5,32,1536]{3,2,1,0:T(8,128)(2,1)} %all_to_all.15), kind=kOutput, calls=%fused_computation.58 | convolution fusion | flops 4032430080 | bytes 26214400 | tf_op jit(solution)/shard_map/sjch,jhd->sjcd/dot_general | solution.py:156
  394.9 4.5 copy.70
  399.4 5.4 %all-to-all-start.2 = ((bf16[8,5,32,1536]{3,2,1,0:T(8,128)(2,1)}), bf16[8,5,32,1536]{3,2,1,0:T(8,128)(2,1)}, u32[]{:S(2)}, u32[]{:S(2)}) async-start(bf16[8,5,32,1536]{3,2,1,0:T(8,128)(2,1)} %copy.70), calls=%async_computation.2 | async-start | bytes 7864320 | tf_op jit(solution)/shard_map/all_to_all | solution.py:157
  405.5 45.4 %all-to-all-done.2 = bf16[8,5,32,1536]{3,2,1,0:T(8,128)(2,1)} async-done(((bf16[8,5,32,1536]{3,2,1,0:T(8,128)(2,1)}), bf16[8,5,32,1536]{3,2,1,0:T(8,128)(2,1)}, u32[]{:S(2)}, u32[]{:S(2)}) %all-to-all-start.2) | async-done | bytes 3932192 | tf_op jit(solution)/shard_map/all_to_all | solution.py:157
  450.8 9.9 %gather_fusion = bf16[1024,1536]{1,0:T(8,128)(2,1)} fusion(bf16[1280,1536]{1,0:T(8,128)(2,1)} %bitcast.22, s32[1024]{0:T(1024)S(1)} %broadcast_clamp_fusion), kind=kCustom, calls=%fused_computation | custom fusion | bytes 6295552 | tf_op jit(solution)/shard_map/gather | solution.py:161
  460.7 4.7 fusion.40
  (271 shorter events, 113.6 us)
Async XLA Ops:
  6.5 398.4 %copy-start = (bf16[1536,40]{0,1:T(8,128)(2,1)S(1)}, bf16[1536,40]{0,1:T(8,128)(2,1)}, u32[]{:S(2)}) copy-start(bf16[1536,40]{0,1:T(8,128)(2,1)} %param.23) | copy-start | bytes 368644
  6.5 279.6 %all-gather.3.cloned.1.call-start = ((), (), s32[]{:S(2)}) async-start(), calls=%async_computation.3 | async-start | bytes 4456448 | tf_op jit(solution)/shard_map/all_gather | solution.py:116
  7.8 6.7 %copy-start.7 = (bf16[1,256,1024]{2,1,0:T(8,128)(2,1)S(1)}, bf16[1,256,1024]{2,1,0:T(8,128)(2,1)}, u32[]{:S(2)}) copy-start(bf16[1,256,1024]{2,1,0:T(8,128)(2,1)} %param.20) | copy-start | bytes 1572868
  18.8 8.0 %copy-start.8 = (bf16[5,32,1536]{2,1,0:T(8,128)(2,1)S(1)}, bf16[5,32,1536]{2,1,0:T(8,128)(2,1)}, u32[]{:S(2)}) copy-start(bf16[5,32,1536]{2,1,0:T(8,128)(2,1)} %param.27) | copy-start | bytes 1474564
  18.8 8.0 %copy-start.9 = (bf16[5,32,1536]{2,1,0:T(8,128)(2,1)S(1)}, bf16[5,32,1536]{2,1,0:T(8,128)(2,1)}, u32[]{:S(2)}) copy-start(bf16[5,32,1536]{2,1,0:T(8,128)(2,1)} %param.26) | copy-start | bytes 1474564
  18.8 8.0 %copy-start.10 = (bf16[5,32,1536]{2,1,0:T(8,128)(2,1)S(1)}, bf16[5,32,1536]{2,1,0:T(8,128)(2,1)}, u32[]{:S(2)}) copy-start(bf16[5,32,1536]{2,1,0:T(8,128)(2,1)} %param.25) | copy-start | bytes 1474564
  18.8 9.4 %copy-start.12 = (s32[128,8]{0,1:T(8,128)S(1)}, s32[128,8]{0,1:T(8,128)}, u32[]{:S(2)}) copy-start(s32[128,8]{0,1:T(8,128)} %param.24) | copy-start | bytes 12292
  18.8 155.5 %all-to-all-start = ((bf16[16,256,1024]{2,1,0:T(8,128)(2,1)}), bf16[16,256,1024]{2,1,0:T(8,128)(2,1)}, u32[]{:S(2)}, u32[]{:S(2)}) async-start(bf16[16,256,1024]{2,1,0:T(8,128)(2,1)} %stack.3), calls=%async_computation | async-start | bytes 16777216 | tf_op jit(solution)/shard_map/all_to_all | solution.py:112
  26.6 347.7 %all-gather.5.cloned.1.call-start = ((), (), s32[]{:S(2)}) async-start(), calls=%async_computation.4 | async-start | bytes 25067520 | tf_op jit(solution)/shard_map/all_gather | solution.py:149
  177.1 8.1 %copy-start.3 = (f32[128,8,3,64]{0,3,2,1:T(8,128)S(1)}, f32[128,8,3,64]{0,3,2,1:T(8,128)}, u32[]{:S(2)}) copy-start(f32[128,8,3,64]{0,3,2,1:T(8,128)} %get-tuple-element.423) | copy-start | bytes 2359300 | tf_op jit(solution)/shard_map/while
  190.7 9.0 %copy-start.3 = (f32[128,8,3,64]{0,3,2,1:T(8,128)S(1)}, f32[128,8,3,64]{0,3,2,1:T(8,128)}, u32[]{:S(2)}) copy-start(f32[128,8,3,64]{0,3,2,1:T(8,128)} %get-tuple-element.423) | copy-start | bytes 2359300 | tf_op jit(solution)/shard_map/while
  194.5 6.1 %copy-start.1 = (f32[8,512,128,3]{2,1,3,0:T(8,128)S(1)}, f32[8,512,128,3]{2,1,3,0:T(8,128)}, u32[]{:S(2)}) copy-start(f32[8,512,128,3]{2,1,3,0:T(8,128)} %get-tuple-element.405) | copy-start | bytes 18874372 | tf_op jit(solution)/shard_map/while
  205.8 8.2 %copy-start.3 = (f32[128,8,3,64]{0,3,2,1:T(8,128)S(1)}, f32[128,8,3,64]{0,3,2,1:T(8,128)}, u32[]{:S(2)}) copy-start(f32[128,8,3,64]{0,3,2,1:T(8,128)} %get-tuple-element.423) | copy-start | bytes 2359300 | tf_op jit(solution)/shard_map/while
  209.6 4.8 %copy-start.1 = (f32[8,512,128,3]{2,1,3,0:T(8,128)S(1)}, f32[8,512,128,3]{2,1,3,0:T(8,128)}, u32[]{:S(2)}) copy-start(f32[8,512,128,3]{2,1,3,0:T(8,128)} %get-tuple-element.405) | copy-start | bytes 18874372 | tf_op jit(solution)/shard_map/while
  219.6 8.1 %copy-start.3 = (f32[128,8,3,64]{0,3,2,1:T(8,128)S(1)}, f32[128,8,3,64]{0,3,2,1:T(8,128)}, u32[]{:S(2)}) copy-start(f32[128,8,3,64]{0,3,2,1:T(8,128)} %get-tuple-element.423) | copy-start | bytes 2359300 | tf_op jit(solution)/shard_map/while
  233.2 8.8 %copy-start.3 = (f32[128,8,3,64]{0,3,2,1:T(8,128)S(1)}, f32[128,8,3,64]{0,3,2,1:T(8,128)}, u32[]{:S(2)}) copy-start(f32[128,8,3,64]{0,3,2,1:T(8,128)} %get-tuple-element.423) | copy-start | bytes 2359300 | tf_op jit(solution)/shard_map/while
  247.6 8.2 %copy-start.3 = (f32[128,8,3,64]{0,3,2,1:T(8,128)S(1)}, f32[128,8,3,64]{0,3,2,1:T(8,128)}, u32[]{:S(2)}) copy-start(f32[128,8,3,64]{0,3,2,1:T(8,128)} %get-tuple-element.423) | copy-start | bytes 2359300 | tf_op jit(solution)/shard_map/while
  251.4 4.9 %copy-start.1 = (f32[8,512,128,3]{2,1,3,0:T(8,128)S(1)}, f32[8,512,128,3]{2,1,3,0:T(8,128)}, u32[]{:S(2)}) copy-start(f32[8,512,128,3]{2,1,3,0:T(8,128)} %get-tuple-element.405) | copy-start | bytes 18874372 | tf_op jit(solution)/shard_map/while
  261.5 8.1 %copy-start.3 = (f32[128,8,3,64]{0,3,2,1:T(8,128)S(1)}, f32[128,8,3,64]{0,3,2,1:T(8,128)}, u32[]{:S(2)}) copy-start(f32[128,8,3,64]{0,3,2,1:T(8,128)} %get-tuple-element.423) | copy-start | bytes 2359300 | tf_op jit(solution)/shard_map/while
  265.3 4.7 copy-start.1
  275.1 8.3 %copy-start.3 = (f32[128,8,3,64]{0,3,2,1:T(8,128)S(1)}, f32[128,8,3,64]{0,3,2,1:T(8,128)}, u32[]{:S(2)}) copy-start(f32[128,8,3,64]{0,3,2,1:T(8,128)} %get-tuple-element.423) | copy-start | bytes 2359300 | tf_op jit(solution)/shard_map/while
  279.0 4.8 %copy-start.1 = (f32[8,512,128,3]{2,1,3,0:T(8,128)S(1)}, f32[8,512,128,3]{2,1,3,0:T(8,128)}, u32[]{:S(2)}) copy-start(f32[8,512,128,3]{2,1,3,0:T(8,128)} %get-tuple-element.405) | copy-start | bytes 18874372 | tf_op jit(solution)/shard_map/while
  286.1 29.4 %copy-start.2 = (bf16[128,1536]{1,0:T(8,128)(2,1)S(1)}, bf16[128,1536]{1,0:T(8,128)(2,1)}, u32[]{:S(2)}) copy-start(bf16[128,1536]{1,0:T(8,128)(2,1)} %param.16) | copy-start | bytes 1179652
  399.4 51.4 %all-to-all-start.2 = ((bf16[8,5,32,1536]{3,2,1,0:T(8,128)(2,1)}), bf16[8,5,32,1536]{3,2,1,0:T(8,128)(2,1)}, u32[]{:S(2)}, u32[]{:S(2)}) async-start(bf16[8,5,32,1536]{3,2,1,0:T(8,128)(2,1)} %copy.70), calls=%async_computation.2 | async-start | bytes 7864320 | tf_op jit(solution)/shard_map/all_to_all | solution.py:157
  (20 other events, 39.0 us)
Sparse Core Ops, SparseCore 0:
  14.5 166.4 all-gather.2
  183.2 148.4 all-gather.4
